TPU v7x, 512 devices: a whole 4x4x16 slice. The times are simulated.
512 devices in a mesh: tm: 32 (over z, core), band: 4 (over y), fsdp: 4 (over x).
Axes of the slice: x: 4, y: 4, z: 16, core: 2. Of those that a mesh axis runs over, the one named last changes fastest.
Arguments:
- video: bfloat16 [128, 64, 128, 256], P('tm', 'band', 'fsdp'), may hold values from -8 to 8
- clip_lengths: int32 [16], replicated, may hold values from 1 to 31, 128 in all
- norm_gains: float32 [2, 256], replicated, may hold values from 0.1 to 1.9
- spatial_kernel_weight: bfloat16 [256, 2304], P(('band', 'fsdp')), may hold values from -0.125 to 0.125
- w_time: bfloat16 [256, 768], P(('band', 'fsdp')), may hold values from -0.21875 to 0.21875
- w_qkv: bfloat16 [256, 768], P(('band', 'fsdp')), may hold values from -4 to 4
- w_out: bfloat16 [256, 256], P(('band', 'fsdp')), may hold values from -0.375 to 0.375
Outputs:
- mixed: bfloat16 [4, 4, 512, 128, 256], P('band', 'fsdp', 'tm')
Inputs may be any that keep to these rules, and one draw needn't show every extreme that they name: `clip_lengths`: every clip has at least one frame and the lengths sum to 128.
All inputs are finite; a program needn't handle non-finite values.
Results may differ from a plain program's by a relative error of at most 0.0064.
Values may be sent and summed in bfloat16 or wider, within the bound.
No kernel may reach another device: no remote copies, remote signals or barrier semaphores. Data moves between devices by JAX's collectives and lax.ppermute only.
A program may use at most 64 MiB of HBM per device.

v0:
```python
import math
import jax
import jax.numpy as jnp
from jax import lax
from jax.sharding import PartitionSpec as P

GROUPS = 32
EPS = 1e-06


def with_halo(x, sides, width):
    for axis, dim in sides:
        size, length = (lax.axis_size(axis), x.shape[dim])
        up = [(i, (i + 1) % size) for i in range(size - 1)]
        down = [(j, i) for i, j in up]
        last = lax.slice_in_dim(x, length - width, length, axis=dim)
        initial = lax.slice_in_dim(x, 0, width, axis=dim)
        before = lax.ppermute(last, axis, up)
        after = lax.ppermute(initial, axis, down)
        x = jnp.concatenate([before, x, after], axis=dim)
    return x


def from_behind(x, axis, by):
    length = lax.axis_size(axis)
    pairs = [(i, i + by) for i in range(length) if 0 <= i + by < length]
    return lax.ppermute(x, axis, pairs)


def butterfly_sum(x, axes):
    for axis in axes:
        size = lax.axis_size(axis)
        step = 1
        while step < size:
            pairs = [(i, i ^ step) for i in range(size)]
            x = x + lax.ppermute(x, axis, pairs)
            step *= 2
    return x


def frame_starts(clip_lengths, total):
    ends = jnp.cumsum(clip_lengths)
    begins = ends - clip_lengths
    index = jnp.arange(total, dtype=jnp.int32)
    chosen = jnp.where(begins[None, :] <= index[:, None], begins[None, :], 0)
    return jnp.max(chosen, axis=1)


def group_moments(field):
    frames, height, width, chans = field.shape
    group_width = chans // GROUPS
    vals = field.astype(jnp.float32).reshape(frames, height * width, GROUPS, group_width)
    sums = jnp.sum(vals, axis=(1, 3))
    squares = jnp.sum(vals * vals, axis=(1, 3))
    both = butterfly_sum(jnp.stack([sums, squares]), ("band", "fsdp"))
    sums, squares = (both[0], both[1])
    count = height * width * group_width * lax.axis_size("band") * lax.axis_size("fsdp")
    mean = sums / count
    scale = lax.rsqrt(squares / count - mean * mean + EPS)
    return (mean, scale)


def apply_norm(field, mean, scale, gain):
    shape = field.shape
    chans = shape[-1]
    group_width = chans // GROUPS
    vals = field.astype(jnp.float32).reshape(shape[0], -1, GROUPS, group_width)
    normed = (vals - mean[:, None, :, None]) * scale[:, None, :, None]
    return normed.reshape(shape) * gain


def body(video, clip_lengths, norm_gains, spatial_kernel_weight, w_time, w_qkv, w_out):
    frames, height, width, chans = video.shape
    widths = [w.shape[1] for w in (spatial_kernel_weight, w_time, w_qkv, w_out)]
    packed = jnp.concatenate([spatial_kernel_weight, w_time, w_qkv, w_out], axis=1)
    gathered = lax.all_gather(packed, ("band", "fsdp"), axis=0, tiled=True)
    offsets = [sum(widths[:i]) for i in range(4)]
    space_full, time_full, qkv_full, output_complete = [
        gathered[:, o : o + w] for o, w in zip(offsets, widths)
    ]
    ranks = lax.axis_size("tm")
    total_frames = frames * ranks
    first = lax.axis_index("tm") * frames
    starts = frame_starts(clip_lengths, total_frames)
    local_starts = lax.dynamic_slice_in_dim(starts, first, frames)
    mean_one, scale_one = group_moments(video)
    act = jax.nn.silu(apply_norm(video, mean_one, scale_one, norm_gains[0])).astype(jnp.bfloat16)
    padded = with_halo(act, (("band", 1), ("fsdp", 2)), 1)
    spatial = jnp.zeros((frames, height, width, chans), jnp.float32)
    for tap in range(9):
        shift_y = tap // 3
        shift_x = tap % 3
        spatial = spatial + jnp.einsum(
            "fhwc,cd->fhwd",
            padded[:, shift_y : shift_y + height, shift_x : shift_x + width],
            space_full[:, tap * chans : (tap + 1) * chans],
            preferred_element_type=jnp.float32,
        )
    spatial = spatial.astype(jnp.bfloat16)
    carried = from_behind(spatial[frames - 2 :], "tm", 1)
    extended = jnp.concatenate([carried, spatial], axis=0)
    position = first + jnp.arange(frames, dtype=jnp.int32)
    slots = jnp.arange(frames + 2, dtype=jnp.int32)
    temporal = jnp.zeros((frames, height, width, chans), jnp.float32)
    for tap in range(3):
        source = jnp.maximum(position - 2 + tap, local_starts) - first + 2
        select = (source[:, None] == slots[None, :]).astype(jnp.bfloat16)
        picked = jnp.einsum(
            "fe,ehwc->fhwc", select, extended, preferred_element_type=jnp.float32
        ).astype(jnp.bfloat16)
        temporal = temporal + jnp.einsum(
            "fhwc,cd->fhwd",
            picked,
            time_full[:, tap * chans : (tap + 1) * chans],
            preferred_element_type=jnp.float32,
        )
    resid = (video.astype(jnp.float32) + temporal).astype(jnp.bfloat16)
    pixels = height * width
    group_pixels = pixels // ranks
    flat_resid = resid.reshape(frames, ranks, group_pixels, chans).transpose(1, 0, 2, 3)
    received = lax.all_to_all(flat_resid, "tm", split_axis=0, concat_axis=0, tiled=True)
    resid_time = received.reshape(total_frames, group_pixels, chans)
    mean_two, scale_two = group_moments(resid)
    mine = jnp.concatenate([mean_two, scale_two], axis=1)
    big = jnp.pad(mine, ((0, 8 - frames), (0, 1024 - 2 * GROUPS)))
    moments = lax.all_gather(big, "tm", axis=0, tiled=True).reshape(ranks, 8, 1024)[
        :, :frames, : 2 * GROUPS
    ]
    moments = moments.reshape(total_frames, 2 * GROUPS)
    mean_all, scale_all = (moments[:, :GROUPS], moments[:, GROUPS:])
    flat_norm = apply_norm(resid_time, mean_all, scale_all, norm_gains[1]).astype(jnp.bfloat16)
    qkv_time = jnp.einsum(
        "fpc,cd->fpd", flat_norm, qkv_full, preferred_element_type=jnp.float32
    ).astype(jnp.bfloat16)
    query = qkv_time[..., :chans]
    keys = qkv_time[..., chans : 2 * chans]
    value_rows = qkv_time[..., 2 * chans :]
    index = jnp.arange(total_frames, dtype=jnp.int32)
    allowed = (index[None, :] <= index[:, None]) & (index[None, :] >= starts[:, None])
    scores = jnp.einsum(
        "fpc,gpc->pfg", query, keys, preferred_element_type=jnp.float32
    ) / math.sqrt(chans)
    scores = jnp.where(allowed[None], scores, -1e30)
    top = jnp.max(scores, axis=-1, keepdims=True)
    expo = jnp.where(allowed[None], jnp.exp(scores - top), 0.0)
    attention_probabilities = (expo / jnp.sum(expo, axis=-1, keepdims=True)).astype(jnp.bfloat16)
    attention_output = jnp.einsum(
        "boh,hba->boa", attention_probabilities, value_rows, preferred_element_type=jnp.float32
    ).astype(jnp.bfloat16)
    projected_output = jnp.einsum(
        "axi,iy->axy", attention_output, output_complete, preferred_element_type=jnp.float32
    )
    mixed = (jnp.swapaxes(resid_time, 0, 1).astype(jnp.float32) + projected_output).astype(
        jnp.bfloat16
    )
    return mixed.reshape(1, 1, mixed.shape[0], total_frames, chans)


def solution(mesh):
    return jax.shard_map(
        body,
        mesh=mesh,
        in_specs=(
            P("tm", "band", "fsdp", None),
            P(),
            P(),
            P(("band", "fsdp"), None),
            P(("band", "fsdp"), None),
            P(("band", "fsdp"), None),
            P(("band", "fsdp"), None),
        ),
        out_specs=P("band", "fsdp", "tm", None, None),
        check_vma=False,
    )
```

profile of v0, /device:TPU:1, one launch (start us, length us, event | category | flops | bytes accessed | tf_op | source)
XLA Modules:
  0.0 233.3 jit_solution(3845554850148898094)
XLA Ops:
  10.2 4.0 %collective-permute-start = (f32[2,4,32]{2,1,0:T(4,128)S(1)}, f32[2,4,32]{2,1,0:T(4,128)S(1)}, u32[]{:S(2)}, u32[]{:S(2)}) collective-permute-start(f32[2,4,32]{2,1,0:T(4,128)S(1)} %pad_maximum_fusion.6), channel_id=1, source_target_pairs={{0,4},{4,0},{8,12},{12,8},{1,5},{5,1},{9,13},{13,9},{2,6},{6,2},{1... | collective-permute-start | bytes 3080 | tf_op jit(solution)/shard_map/ppermute | solution.py:36
  15.2 5.0 %collective-permute-start.1 = (f32[2,4,32]{2,1,0:T(4,128)S(1)}, f32[2,4,32]{2,1,0:T(4,128)S(1)}, u32[]{:S(2)}, u32[]{:S(2)}) collective-permute-start(f32[2,4,32]{2,1,0:T(4,128)S(1)} %fusion.93), channel_id=1, source_target_pairs={{0,8},{4,12},{8,0},{12,4},{1,9},{5,13},{9,1},{13,5},{2,10},{6,14},... | collective-permute-start | bytes 3080 | tf_op jit(solution)/shard_map/ppermute | solution.py:36
  21.2 3.2 %collective-permute-start.2 = (f32[2,4,32]{2,1,0:T(4,128)S(1)}, f32[2,4,32]{2,1,0:T(4,128)S(1)}, u32[]{:S(2)}, u32[]{:S(2)}) collective-permute-start(f32[2,4,32]{2,1,0:T(4,128)S(1)} %fusion.104), channel_id=1, source_target_pairs={{0,1},{1,0},{2,3},{3,2},{4,5},{5,4},{6,7},{7,6},{8,9},{9,8},{10,11... | collective-permute-start | bytes 3080 | tf_op jit(solution)/shard_map/ppermute | solution.py:36
  25.5 4.7 %collective-permute-start.3 = (f32[2,4,32]{2,1,0:T(4,128)S(1)}, f32[2,4,32]{2,1,0:T(4,128)S(1)}, u32[]{:S(2)}, u32[]{:S(2)}) collective-permute-start(f32[2,4,32]{2,1,0:T(4,128)S(1)} %add.111), channel_id=1, source_target_pairs={{0,2},{1,3},{2,0},{3,1},{4,6},{5,7},{6,4},{7,5},{8,10},{9,11},{10,... | collective-permute-start | bytes 3080 | tf_op jit(solution)/shard_map/ppermute | solution.py:36
  32.4 3.2 %collective-permute-start.4 = (bf16[4,1,32,256]{3,2,1,0:T(8,128)(2,1)S(1)}, bf16[4,1,32,256]{3,2,1,0:T(8,128)(2,1)S(1)}, u32[]{:S(2)}, u32[]{:S(2)}) collective-permute-start(bf16[4,1,32,256]{3,2,1,0:T(8,128)(2,1)S(1)} %get-tuple-element.13), channel_id=1, source_target_pairs={{0,4},{4,8},{8,12},{1,5},{5,9},{9,13},{2,6},{6,10},{10,14},{3,7},{... | collective-permute-start | bytes 196616 | tf_op jit(solution)/shard_map/ppermute | solution.py:18
  37.0 4.1 %collective-permute-done.5 = bf16[4,1,32,256]{3,2,1,0:T(8,128)(2,1)S(1)} collective-permute-done((bf16[4,1,32,256]{3,2,1,0:T(8,128)(2,1)S(1)}, bf16[4,1,32,256]{3,2,1,0:T(8,128)(2,1)S(1)}, u32[]{:S(2)}, u32[]{:S(2)}) %collective-permute-start.5) | collective-permute-done | bytes 65568 | tf_op jit(solution)/shard_map/ppermute | solution.py:19
  41.3 3.2 %collective-permute-start.6 = (bf16[4,18,1,256]{3,2,1,0:T(2,128)(2,1)S(1)}, bf16[4,18,1,256]{3,2,1,0:T(2,128)(2,1)S(1)}, u32[]{:S(2)}, u32[]{:S(2)}) collective-permute-start(bf16[4,18,1,256]{3,2,1,0:T(2,128)(2,1)S(1)} %get-tuple-element.12), channel_id=1, source_target_pairs={{0,1},{1,2},{2,3},{4,5},{5,6},{6,7},{8,9},{9,10},{10,11},{12,13},{... | collective-permute-start | bytes 110600 | tf_op jit(solution)/shard_map/ppermute | solution.py:18
  45.9 3.7 %collective-permute-done.7 = bf16[4,18,1,256]{3,2,1,0:T(2,128)(2,1)S(1)} collective-permute-done((bf16[4,18,1,256]{3,2,1,0:T(2,128)(2,1)S(1)}, bf16[4,18,1,256]{3,2,1,0:T(2,128)(2,1)S(1)}, u32[]{:S(2)}, u32[]{:S(2)}) %collective-permute-start.7) | collective-permute-done | bytes 36896 | tf_op jit(solution)/shard_map/ppermute | solution.py:19
  51.3 23.3 %all-gather.3.cloned.1.call-done = bf16[256,4096]{1,0:T(8,128)(2,1)} async-done(((bf16[16,4096]{1,0:T(8,128)(2,1)}), bf16[256,4096]{1,0:T(8,128)(2,1)}) %all-gather.3.cloned.1.call-update) | async-done | bytes 2097168 | tf_op jit(solution)/shard_map/all_gather | solution.py:76
  81.5 5.3 %collective-permute-start.8 = (bf16[2,16,32,256]{3,2,1,0:T(8,128)(2,1)S(1)}, bf16[2,16,32,256]{3,2,1,0:T(8,128)(2,1)S(1)}, u32[]{:S(2)}, u32[]{:S(2)}) collective-permute-start(bf16[2,16,32,256]{3,2,1,0:T(8,128)(2,1)S(1)} %slice.197), channel_id=1, source_target_pairs={{0,16},{16,32},{32,48},{48,64},{64,80},{80,96},{96,112},{112,128},... | collective-permute-start | bytes 1572872 | tf_op jit(solution)/shard_map/ppermute | solution.py:27
  87.2 5.7 %collective-permute-done.8 = bf16[2,16,32,256]{3,2,1,0:T(8,128)(2,1)S(1)} collective-permute-done((bf16[2,16,32,256]{3,2,1,0:T(8,128)(2,1)S(1)}, bf16[2,16,32,256]{3,2,1,0:T(8,128)(2,1)S(1)}, u32[]{:S(2)}, u32[]{:S(2)}) %collective-permute-start.8) | collective-permute-done | bytes 524320 | tf_op jit(solution)/shard_map/ppermute | solution.py:27
  102.3 15.1 %all-to-all-start = ((bf16[32,4,16,256]{3,2,1,0:T(8,128)(2,1)}), bf16[32,4,16,256]{3,2,1,0:T(8,128)(2,1)S(1)}, u32[]{:S(2)}, u32[]{:S(2)}) async-start(bf16[32,4,16,256]{3,2,1,0:T(8,128)(2,1)} %bitcast.135), calls=%async_computation | async-start | bytes 2097152 | tf_op jit(solution)/shard_map/all_to_all | solution.py:121
  117.8 2.8 %collective-permute-start.9 = (f32[2,4,32]{2,1,0:T(4,128)S(1)}, f32[2,4,32]{2,1,0:T(4,128)S(1)}, u32[]{:S(2)}, u32[]{:S(2)}) collective-permute-start(f32[2,4,32]{2,1,0:T(4,128)S(1)} %pad_maximum_fusion.7), channel_id=1, source_target_pairs={{0,4},{4,0},{8,12},{12,8},{1,5},{5,1},{9,13},{13,9},{2,6},{6,2},{1... | collective-permute-start | bytes 3080 | tf_op jit(solution)/shard_map/ppermute | solution.py:36
  120.6 1.8 collective-permute-done.9
  122.5 3.7 %collective-permute-start.10 = (f32[2,4,32]{2,1,0:T(4,128)S(1)}, f32[2,4,32]{2,1,0:T(4,128)S(1)}, u32[]{:S(2)}, u32[]{:S(2)}) collective-permute-start(f32[2,4,32]{2,1,0:T(4,128)S(1)} %fusion.92), channel_id=1, source_target_pairs={{0,8},{4,12},{8,0},{12,4},{1,9},{5,13},{9,1},{13,5},{2,10},{6,14},... | collective-permute-start | bytes 3080 | tf_op jit(solution)/shard_map/ppermute | solution.py:36
  126.2 2.4 %collective-permute-done.10 = f32[2,4,32]{2,1,0:T(4,128)S(1)} collective-permute-done((f32[2,4,32]{2,1,0:T(4,128)S(1)}, f32[2,4,32]{2,1,0:T(4,128)S(1)}, u32[]{:S(2)}, u32[]{:S(2)}) %collective-permute-start.10) | collective-permute-done | bytes 1056 | tf_op jit(solution)/shard_map/ppermute | solution.py:36
  128.6 2.8 %collective-permute-start.11 = (f32[2,4,32]{2,1,0:T(4,128)S(1)}, f32[2,4,32]{2,1,0:T(4,128)S(1)}, u32[]{:S(2)}, u32[]{:S(2)}) collective-permute-start(f32[2,4,32]{2,1,0:T(4,128)S(1)} %fusion.103), channel_id=1, source_target_pairs={{0,1},{1,0},{2,3},{3,2},{4,5},{5,4},{6,7},{7,6},{8,9},{9,8},{10,11... | collective-permute-start | bytes 3080 | tf_op jit(solution)/shard_map/ppermute | solution.py:36
  131.4 1.8 collective-permute-done.11
  133.2 3.7 %collective-permute-start.12 = (f32[2,4,32]{2,1,0:T(4,128)S(1)}, f32[2,4,32]{2,1,0:T(4,128)S(1)}, u32[]{:S(2)}, u32[]{:S(2)}) collective-permute-start(f32[2,4,32]{2,1,0:T(4,128)S(1)} %add.132), channel_id=1, source_target_pairs={{0,2},{1,3},{2,0},{3,1},{4,6},{5,7},{6,4},{7,5},{8,10},{9,11},{10,... | collective-permute-start | bytes 3080 | tf_op jit(solution)/shard_map/ppermute | solution.py:36
  137.0 2.4 %collective-permute-done.12 = f32[2,4,32]{2,1,0:T(4,128)S(1)} collective-permute-done((f32[2,4,32]{2,1,0:T(4,128)S(1)}, f32[2,4,32]{2,1,0:T(4,128)S(1)}, u32[]{:S(2)}, u32[]{:S(2)}) %collective-permute-start.12) | collective-permute-done | bytes 1056 | tf_op jit(solution)/shard_map/ppermute | solution.py:36
  140.1 73.9 %all-gather.5.cloned.1.call-done = f32[256,1024]{1,0:T(8,128)} async-done(((f32[8,1024]{1,0:T(8,128)}), f32[256,1024]{1,0:T(8,128)}) %all-gather.5.cloned.1.call-update) | async-done | bytes 1048592 | tf_op jit(solution)/shard_map/all_gather | solution.py:126
  215.8 4.6 %convolution_convert_fusion = bf16[128,16,768]{2,0,1:T(8,128)(2,1)} fusion(f32[128,16,256]{2,1,0:T(8,128)S(1)} %bitcast_convert_fusion, f32[256]{0:T(256)S(1)} %bitcast.150, f32[128,256]{1,0:T(8,128)S(1)} %copy.42, f32[128,256]{1,0:T(8,128)S(1)} %copy.40, bf16[256,4096]{1,0:T(8,128)(2,1)} %all-gather.3.cloned.1.call-done), kind=kOutput, calls=%fused_computation.7 | convolution fusion | flops 808976384 | bytes 5899264 | tf_op jit(solution)/shard_map/fpc,cd->fpd/dot_general | solution.py:132
  220.4 2.1 fusion.97
  222.5 3.9 %fusion.31 = bf16[1,1,16,128,256]{4,3,2,1,0:T(8,128)(2,1)} fusion(f32[128,16,256]{2,1,0:T(8,128)S(1)} %bitcast_convert_fusion, bf16[128,16,768]{2,0,1:T(8,128)(2,1)} %convolution_convert_fusion, f32[16,128,128]{1,2,0:T(8,128)S(1)} %get-tuple-element.24, f32[16,128]{1,0:T(8,128)S(1)} %get-tuple-element.23, bf16[256,4096]{1,0:T(8,128)(2,1)} %all-gather.3.cloned.1.call-done), kind=kOutput, calls=%fused_computation.39 | convolution fusion | flops 404750336 | bytes 5382144 | tf_op jit(solution)/shard_map/axi,iy->axy/dot_general | solution.py:150
  (91 shorter events, 33.0 us)
Async XLA Ops:
  6.5 25.2 %copy-start.1 = (bf16[4,16,32,256]{3,2,1,0:T(8,128)(2,1)S(1)}, bf16[4,16,32,256]{3,2,1,0:T(8,128)(2,1)}, u32[]{:S(2)}) copy-start(bf16[4,16,32,256]{3,2,1,0:T(8,128)(2,1)} %param.7) | copy-start | bytes 3145732
  6.5 68.1 %all-gather.3.cloned.1.call-start = ((), (), s32[]{:S(2)}) async-start(), calls=%async_computation.1 | async-start | bytes 2228224 | tf_op jit(solution)/shard_map/all_gather | solution.py:76
  10.2 5.0 %collective-permute-start = (f32[2,4,32]{2,1,0:T(4,128)S(1)}, f32[2,4,32]{2,1,0:T(4,128)S(1)}, u32[]{:S(2)}, u32[]{:S(2)}) collective-permute-start(f32[2,4,32]{2,1,0:T(4,128)S(1)} %pad_maximum_fusion.6), channel_id=1, source_target_pairs={{0,4},{4,0},{8,12},{12,8},{1,5},{5,1},{9,13},{13,9},{2,6},{6,2},{1... | collective-permute-start | bytes 3080 | tf_op jit(solution)/shard_map/ppermute | solution.py:36
  15.2 6.0 %collective-permute-start.1 = (f32[2,4,32]{2,1,0:T(4,128)S(1)}, f32[2,4,32]{2,1,0:T(4,128)S(1)}, u32[]{:S(2)}, u32[]{:S(2)}) collective-permute-start(f32[2,4,32]{2,1,0:T(4,128)S(1)} %fusion.93), channel_id=1, source_target_pairs={{0,8},{4,12},{8,0},{12,4},{1,9},{5,13},{9,1},{13,5},{2,10},{6,14},... | collective-permute-start | bytes 3080 | tf_op jit(solution)/shard_map/ppermute | solution.py:36
  21.2 4.3 %collective-permute-start.2 = (f32[2,4,32]{2,1,0:T(4,128)S(1)}, f32[2,4,32]{2,1,0:T(4,128)S(1)}, u32[]{:S(2)}, u32[]{:S(2)}) collective-permute-start(f32[2,4,32]{2,1,0:T(4,128)S(1)} %fusion.104), channel_id=1, source_target_pairs={{0,1},{1,0},{2,3},{3,2},{4,5},{5,4},{6,7},{7,6},{8,9},{9,8},{10,11... | collective-permute-start | bytes 3080 | tf_op jit(solution)/shard_map/ppermute | solution.py:36
  25.5 5.8 %collective-permute-start.3 = (f32[2,4,32]{2,1,0:T(4,128)S(1)}, f32[2,4,32]{2,1,0:T(4,128)S(1)}, u32[]{:S(2)}, u32[]{:S(2)}) collective-permute-start(f32[2,4,32]{2,1,0:T(4,128)S(1)} %add.111), channel_id=1, source_target_pairs={{0,2},{1,3},{2,0},{3,1},{4,6},{5,7},{6,4},{7,5},{8,10},{9,11},{10,... | collective-permute-start | bytes 3080 | tf_op jit(solution)/shard_map/ppermute | solution.py:36
  32.4 4.6 %collective-permute-start.4 = (bf16[4,1,32,256]{3,2,1,0:T(8,128)(2,1)S(1)}, bf16[4,1,32,256]{3,2,1,0:T(8,128)(2,1)S(1)}, u32[]{:S(2)}, u32[]{:S(2)}) collective-permute-start(bf16[4,1,32,256]{3,2,1,0:T(8,128)(2,1)S(1)} %get-tuple-element.13), channel_id=1, source_target_pairs={{0,4},{4,8},{8,12},{1,5},{5,9},{9,13},{2,6},{6,10},{10,14},{3,7},{... | collective-permute-start | bytes 196616 | tf_op jit(solution)/shard_map/ppermute | solution.py:18
  35.7 5.4 %collective-permute-start.5 = (bf16[4,1,32,256]{3,2,1,0:T(8,128)(2,1)S(1)}, bf16[4,1,32,256]{3,2,1,0:T(8,128)(2,1)S(1)}, u32[]{:S(2)}, u32[]{:S(2)}) collective-permute-start(bf16[4,1,32,256]{3,2,1,0:T(8,128)(2,1)S(1)} %get-tuple-element.14), channel_id=1, source_target_pairs={{4,0},{8,4},{12,8},{5,1},{9,5},{13,9},{6,2},{10,6},{14,10},{7,3},{... | collective-permute-start | bytes 196616 | tf_op jit(solution)/shard_map/ppermute | solution.py:19
  41.3 4.6 %collective-permute-start.6 = (bf16[4,18,1,256]{3,2,1,0:T(2,128)(2,1)S(1)}, bf16[4,18,1,256]{3,2,1,0:T(2,128)(2,1)S(1)}, u32[]{:S(2)}, u32[]{:S(2)}) collective-permute-start(bf16[4,18,1,256]{3,2,1,0:T(2,128)(2,1)S(1)} %get-tuple-element.12), channel_id=1, source_target_pairs={{0,1},{1,2},{2,3},{4,5},{5,6},{6,7},{8,9},{9,10},{10,11},{12,13},{... | collective-permute-start | bytes 110600 | tf_op jit(solution)/shard_map/ppermute | solution.py:18
  44.5 5.1 %collective-permute-start.7 = (bf16[4,18,1,256]{3,2,1,0:T(2,128)(2,1)S(1)}, bf16[4,18,1,256]{3,2,1,0:T(2,128)(2,1)S(1)}, u32[]{:S(2)}, u32[]{:S(2)}) collective-permute-start(bf16[4,18,1,256]{3,2,1,0:T(2,128)(2,1)S(1)} %get-tuple-element.11), channel_id=1, source_target_pairs={{1,0},{2,1},{3,2},{5,4},{6,5},{7,6},{9,8},{10,9},{11,10},{13,12},{... | collective-permute-start | bytes 110600 | tf_op jit(solution)/shard_map/ppermute | solution.py:19
  74.6 1.7 copy-start.3
  76.3 1.4 copy-start
  80.4 6.4 %copy-start.4 = (s32[16]{0:T(128)S(1)}, s32[16]{0:T(128)}, u32[]{:S(2)}) copy-start(s32[16]{0:T(128)} %param.8) | copy-start | bytes 196
  81.5 11.4 %collective-permute-start.8 = (bf16[2,16,32,256]{3,2,1,0:T(8,128)(2,1)S(1)}, bf16[2,16,32,256]{3,2,1,0:T(8,128)(2,1)S(1)}, u32[]{:S(2)}, u32[]{:S(2)}) collective-permute-start(bf16[2,16,32,256]{3,2,1,0:T(8,128)(2,1)S(1)} %slice.197), channel_id=1, source_target_pairs={{0,16},{16,32},{32,48},{48,64},{64,80},{80,96},{96,112},{112,128},... | collective-permute-start | bytes 1572872 | tf_op jit(solution)/shard_map/ppermute | solution.py:27
  98.0 1.4 copy-start.2
  102.3 113.1 %all-to-all-start = ((bf16[32,4,16,256]{3,2,1,0:T(8,128)(2,1)}), bf16[32,4,16,256]{3,2,1,0:T(8,128)(2,1)S(1)}, u32[]{:S(2)}, u32[]{:S(2)}) async-start(bf16[32,4,16,256]{3,2,1,0:T(8,128)(2,1)} %bitcast.135), calls=%async_computation | async-start | bytes 2097152 | tf_op jit(solution)/shard_map/all_to_all | solution.py:121
  117.4 96.7 %all-gather.5.cloned.1.call-start = ((), (), s32[]{:S(2)}) async-start(), calls=%async_computation.2 | async-start | bytes 1081344 | tf_op jit(solution)/shard_map/all_gather | solution.py:126
  117.8 4.6 %collective-permute-start.9 = (f32[2,4,32]{2,1,0:T(4,128)S(1)}, f32[2,4,32]{2,1,0:T(4,128)S(1)}, u32[]{:S(2)}, u32[]{:S(2)}) collective-permute-start(f32[2,4,32]{2,1,0:T(4,128)S(1)} %pad_maximum_fusion.7), channel_id=1, source_target_pairs={{0,4},{4,0},{8,12},{12,8},{1,5},{5,1},{9,13},{13,9},{2,6},{6,2},{1... | collective-permute-start | bytes 3080 | tf_op jit(solution)/shard_map/ppermute | solution.py:36
  122.5 6.1 %collective-permute-start.10 = (f32[2,4,32]{2,1,0:T(4,128)S(1)}, f32[2,4,32]{2,1,0:T(4,128)S(1)}, u32[]{:S(2)}, u32[]{:S(2)}) collective-permute-start(f32[2,4,32]{2,1,0:T(4,128)S(1)} %fusion.92), channel_id=1, source_target_pairs={{0,8},{4,12},{8,0},{12,4},{1,9},{5,13},{9,1},{13,5},{2,10},{6,14},... | collective-permute-start | bytes 3080 | tf_op jit(solution)/shard_map/ppermute | solution.py:36
  128.6 4.6 %collective-permute-start.11 = (f32[2,4,32]{2,1,0:T(4,128)S(1)}, f32[2,4,32]{2,1,0:T(4,128)S(1)}, u32[]{:S(2)}, u32[]{:S(2)}) collective-permute-start(f32[2,4,32]{2,1,0:T(4,128)S(1)} %fusion.103), channel_id=1, source_target_pairs={{0,1},{1,0},{2,3},{3,2},{4,5},{5,4},{6,7},{7,6},{8,9},{9,8},{10,11... | collective-permute-start | bytes 3080 | tf_op jit(solution)/shard_map/ppermute | solution.py:36
  133.2 6.1 %collective-permute-start.12 = (f32[2,4,32]{2,1,0:T(4,128)S(1)}, f32[2,4,32]{2,1,0:T(4,128)S(1)}, u32[]{:S(2)}, u32[]{:S(2)}) collective-permute-start(f32[2,4,32]{2,1,0:T(4,128)S(1)} %add.132), channel_id=1, source_target_pairs={{0,2},{1,3},{2,0},{3,1},{4,6},{5,7},{6,4},{7,5},{8,10},{9,11},{10,... | collective-permute-start | bytes 3080 | tf_op jit(solution)/shard_map/ppermute | solution.py:36
Sparse Core Ops, SparseCore 0:
  10.3 64.2 all-gather.2
  140.2 73.7 all-gather.4
where the time goes:
time: 234 us; the launch traced here: 233 us
  waiting for transfers between devices  123 us (53%)
  starting transfers between devices  59.3 us (25%)
  matrix products  24.5 us (10%)
  between operations  13.8 us (6%)
  other arithmetic  7.72 us (3%)
  local copies, waits for them, and re-layouts  5.18 us (2%)
    all_gather x1, waiting for transfers between devices, body(): lax.all_gather(big, 'tm', axis=0, tiled=True).reshape(ranks, 8, 1024)  73.9 us
    ppermute x8, starting transfers between devices, butterfly_sum(): x = x + lax.ppermute(x, axis, pairs)  29.9 us
    all_gather x1, waiting for transfers between devices, body(): gathered = lax.all_gather(packed, ('band', 'fsdp'), axis=0, tiled=True)  23.3 us
    all_to_all x1, starting transfers between devices, body(): lax.all_to_all(flat_resid, 'tm', split_axis=0, concat_axis=0, tiled=True)  15.1 us
    ppermute x8, waiting for transfers between devices, butterfly_sum(): x = x + lax.ppermute(x, axis, pairs)  12 us
    ppermute x2, waiting for transfers between devices, with_halo(): after = lax.ppermute(initial, axis, down)  7.84 us
    ppermute x2, starting transfers between devices, with_halo(): before = lax.ppermute(last, axis, up)  6.45 us
    dot_general x9, matrix products, body(): jnp.einsum('fhwc,cd->fhwd', padded[:, shift_y:shift_y + height, shift_x:s...  5.7 us
  transfers between devices with their start and end apart: 16, of which 14 were waited for; matrix products, arithmetic and copies ran while one was open for 4% of the time, Pallas kernels for 0%

commit v1 on v0

--- a/solution.py
+++ b/solution.py
@@ -123,9 +123,9 @@
     mean_two, scale_two = group_moments(resid)
     mine = jnp.concatenate([mean_two, scale_two], axis=1)
     big = jnp.pad(mine, ((0, 8 - frames), (0, 1024 - 2 * GROUPS)))
-    moments = lax.all_gather(big, "tm", axis=0, tiled=True).reshape(ranks, 8, 1024)[
-        :, :frames, : 2 * GROUPS
-    ]
+    moments = jnp.concatenate(
+        lax.all_to_all(jnp.stack([big] * lax.axis_size("tm")), "tm", 0, 0), axis=0
+    ).reshape(ranks, 8, 1024)[:, :frames, : 2 * GROUPS]
     moments = moments.reshape(total_frames, 2 * GROUPS)
     mean_all, scale_all = (moments[:, :GROUPS], moments[:, GROUPS:])
     flat_norm = apply_norm(resid_time, mean_all, scale_all, norm_gains[1]).astype(jnp.bfloat16)

time: 234 us -> 255 us (1.090)
  waiting for transfers between devices: 123 us -> 138 us
  starting transfers between devices: 59.3 us -> 64 us
    all_gather x1 -> x0, waiting for transfers between devices: 73.9 us -> none  [body(): lax.all_gather(big, 'tm', axis=0, tiled=True).reshape(ranks, 8, 1024)]
    all_to_all x0 -> x1, waiting for transfers between devices: none -> 55.4 us  [body(): lax.all_to_all(jnp.stack([big] * lax.axis_size('tm')), 'tm', 0, 0)]
    all_to_all x1, waiting for transfers between devices: 0.01 us -> 33.6 us  [body(): lax.all_to_all(flat_resid, 'tm', split_axis=0, concat_axis=0, tiled=True)]
    all_to_all x0 -> x1, starting transfers between devices: none -> 4.76 us  [body(): lax.all_to_all(jnp.stack([big] * lax.axis_size('tm')), 'tm', 0, 0)]
  transfers between devices with their start and end apart: 16 -> 16, of which waited for: 14 -> 15; matrix products, arithmetic and copies ran while one was open for 4% -> 3% of each run, Pallas kernels for 0% -> 0%
where the time goes in v1:
time: 255 us; the launch traced here: 254 us
  waiting for transfers between devices  138 us (54%)
  starting transfers between devices  64 us (25%)
  matrix products  24.5 us (10%)
  between operations  13.8 us (5%)
  other arithmetic  7.12 us (3%)
  local copies, waits for them, and re-layouts  6.26 us (2%)
    all_to_all x1, waiting for transfers between devices, body(): lax.all_to_all(jnp.stack([big] * lax.axis_size('tm')), 'tm', 0, 0)  55.4 us
    all_to_all x1, waiting for transfers between devices, body(): lax.all_to_all(flat_resid, 'tm', split_axis=0, concat_axis=0, tiled=True)  33.6 us
    ppermute x8, starting transfers between devices, butterfly_sum(): x = x + lax.ppermute(x, axis, pairs)  29.9 us
    all_gather x1, waiting for transfers between devices, body(): gathered = lax.all_gather(packed, ('band', 'fsdp'), axis=0, tiled=True)  23.3 us
    all_to_all x1, starting transfers between devices, body(): lax.all_to_all(flat_resid, 'tm', split_axis=0, concat_axis=0, tiled=True)  15.1 us
    ppermute x8, waiting for transfers between devices, butterfly_sum(): x = x + lax.ppermute(x, axis, pairs)  12 us
    ppermute x2, waiting for transfers between devices, with_halo(): after = lax.ppermute(initial, axis, down)  7.84 us
    ppermute x2, starting transfers between devices, with_halo(): before = lax.ppermute(last, axis, up)  6.45 us
  transfers between devices with their start and end apart: 16, of which 15 were waited for; matrix products, arithmetic and copies ran while one was open for 3% of the time, Pallas kernels for 0%

profile of v1, /device:TPU:1, one launch (start us, length us, event | category | flops | bytes accessed | tf_op | source)
XLA Modules:
  0.0 253.6 jit_solution(450490602949746780)
XLA Ops:
  10.2 4.0 %collective-permute-start = (f32[2,4,32]{2,1,0:T(4,128)S(1)}, f32[2,4,32]{2,1,0:T(4,128)S(1)}, u32[]{:S(2)}, u32[]{:S(2)}) collective-permute-start(f32[2,4,32]{2,1,0:T(4,128)S(1)} %pad_maximum_fusion.6), channel_id=1, source_target_pairs={{0,4},{4,0},{8,12},{12,8},{1,5},{5,1},{9,13},{13,9},{2,6},{6,2},{1... | collective-permute-start | bytes 3080 | tf_op jit(solution)/shard_map/ppermute | solution.py:36
  15.2 5.0 %collective-permute-start.1 = (f32[2,4,32]{2,1,0:T(4,128)S(1)}, f32[2,4,32]{2,1,0:T(4,128)S(1)}, u32[]{:S(2)}, u32[]{:S(2)}) collective-permute-start(f32[2,4,32]{2,1,0:T(4,128)S(1)} %fusion.93), channel_id=1, source_target_pairs={{0,8},{4,12},{8,0},{12,4},{1,9},{5,13},{9,1},{13,5},{2,10},{6,14},... | collective-permute-start | bytes 3080 | tf_op jit(solution)/shard_map/ppermute | solution.py:36
  21.2 3.2 %collective-permute-start.2 = (f32[2,4,32]{2,1,0:T(4,128)S(1)}, f32[2,4,32]{2,1,0:T(4,128)S(1)}, u32[]{:S(2)}, u32[]{:S(2)}) collective-permute-start(f32[2,4,32]{2,1,0:T(4,128)S(1)} %fusion.104), channel_id=1, source_target_pairs={{0,1},{1,0},{2,3},{3,2},{4,5},{5,4},{6,7},{7,6},{8,9},{9,8},{10,11... | collective-permute-start | bytes 3080 | tf_op jit(solution)/shard_map/ppermute | solution.py:36
  25.5 4.7 %collective-permute-start.3 = (f32[2,4,32]{2,1,0:T(4,128)S(1)}, f32[2,4,32]{2,1,0:T(4,128)S(1)}, u32[]{:S(2)}, u32[]{:S(2)}) collective-permute-start(f32[2,4,32]{2,1,0:T(4,128)S(1)} %add.111), channel_id=1, source_target_pairs={{0,2},{1,3},{2,0},{3,1},{4,6},{5,7},{6,4},{7,5},{8,10},{9,11},{10,... | collective-permute-start | bytes 3080 | tf_op jit(solution)/shard_map/ppermute | solution.py:36
  32.4 3.2 %collective-permute-start.4 = (bf16[4,1,32,256]{3,2,1,0:T(8,128)(2,1)S(1)}, bf16[4,1,32,256]{3,2,1,0:T(8,128)(2,1)S(1)}, u32[]{:S(2)}, u32[]{:S(2)}) collective-permute-start(bf16[4,1,32,256]{3,2,1,0:T(8,128)(2,1)S(1)} %get-tuple-element.13), channel_id=1, source_target_pairs={{0,4},{4,8},{8,12},{1,5},{5,9},{9,13},{2,6},{6,10},{10,14},{3,7},{... | collective-permute-start | bytes 196616 | tf_op jit(solution)/shard_map/ppermute | solution.py:18
  37.0 4.1 %collective-permute-done.5 = bf16[4,1,32,256]{3,2,1,0:T(8,128)(2,1)S(1)} collective-permute-done((bf16[4,1,32,256]{3,2,1,0:T(8,128)(2,1)S(1)}, bf16[4,1,32,256]{3,2,1,0:T(8,128)(2,1)S(1)}, u32[]{:S(2)}, u32[]{:S(2)}) %collective-permute-start.5) | collective-permute-done | bytes 65568 | tf_op jit(solution)/shard_map/ppermute | solution.py:19
  41.3 3.2 %collective-permute-start.6 = (bf16[4,18,1,256]{3,2,1,0:T(2,128)(2,1)S(1)}, bf16[4,18,1,256]{3,2,1,0:T(2,128)(2,1)S(1)}, u32[]{:S(2)}, u32[]{:S(2)}) collective-permute-start(bf16[4,18,1,256]{3,2,1,0:T(2,128)(2,1)S(1)} %get-tuple-element.12), channel_id=1, source_target_pairs={{0,1},{1,2},{2,3},{4,5},{5,6},{6,7},{8,9},{9,10},{10,11},{12,13},{... | collective-permute-start | bytes 110600 | tf_op jit(solution)/shard_map/ppermute | solution.py:18
  45.9 3.7 %collective-permute-done.7 = bf16[4,18,1,256]{3,2,1,0:T(2,128)(2,1)S(1)} collective-permute-done((bf16[4,18,1,256]{3,2,1,0:T(2,128)(2,1)S(1)}, bf16[4,18,1,256]{3,2,1,0:T(2,128)(2,1)S(1)}, u32[]{:S(2)}, u32[]{:S(2)}) %collective-permute-start.7) | collective-permute-done | bytes 36896 | tf_op jit(solution)/shard_map/ppermute | solution.py:19
  51.3 23.3 %all-gather.2.cloned.1.call-done = bf16[256,4096]{1,0:T(8,128)(2,1)} async-done(((bf16[16,4096]{1,0:T(8,128)(2,1)}), bf16[256,4096]{1,0:T(8,128)(2,1)}) %all-gather.2.cloned.1.call-update) | async-done | bytes 2097168 | tf_op jit(solution)/shard_map/all_gather | solution.py:76
  81.5 5.3 %collective-permute-start.8 = (bf16[2,16,32,256]{3,2,1,0:T(8,128)(2,1)S(1)}, bf16[2,16,32,256]{3,2,1,0:T(8,128)(2,1)S(1)}, u32[]{:S(2)}, u32[]{:S(2)}) collective-permute-start(bf16[2,16,32,256]{3,2,1,0:T(8,128)(2,1)S(1)} %slice.197), channel_id=1, source_target_pairs={{0,16},{16,32},{32,48},{48,64},{64,80},{80,96},{96,112},{112,128},... | collective-permute-start | bytes 1572872 | tf_op jit(solution)/shard_map/ppermute | solution.py:27
  87.2 5.7 %collective-permute-done.8 = bf16[2,16,32,256]{3,2,1,0:T(8,128)(2,1)S(1)} collective-permute-done((bf16[2,16,32,256]{3,2,1,0:T(8,128)(2,1)S(1)}, bf16[2,16,32,256]{3,2,1,0:T(8,128)(2,1)S(1)}, u32[]{:S(2)}, u32[]{:S(2)}) %collective-permute-start.8) | collective-permute-done | bytes 524320 | tf_op jit(solution)/shard_map/ppermute | solution.py:27
  102.3 15.1 %all-to-all-start = ((bf16[32,4,16,256]{3,2,1,0:T(8,128)(2,1)}), bf16[32,4,16,256]{3,2,1,0:T(8,128)(2,1)S(1)}, u32[]{:S(2)}, u32[]{:S(2)}) async-start(bf16[32,4,16,256]{3,2,1,0:T(8,128)(2,1)} %bitcast.134), calls=%async_computation | async-start | bytes 2097152 | tf_op jit(solution)/shard_map/all_to_all | solution.py:121
  117.8 2.8 %collective-permute-start.9 = (f32[2,4,32]{2,1,0:T(4,128)S(1)}, f32[2,4,32]{2,1,0:T(4,128)S(1)}, u32[]{:S(2)}, u32[]{:S(2)}) collective-permute-start(f32[2,4,32]{2,1,0:T(4,128)S(1)} %pad_maximum_fusion.7), channel_id=1, source_target_pairs={{0,4},{4,0},{8,12},{12,8},{1,5},{5,1},{9,13},{13,9},{2,6},{6,2},{1... | collective-permute-start | bytes 3080 | tf_op jit(solution)/shard_map/ppermute | solution.py:36
  122.4 3.7 %collective-permute-start.10 = (f32[2,4,32]{2,1,0:T(4,128)S(1)}, f32[2,4,32]{2,1,0:T(4,128)S(1)}, u32[]{:S(2)}, u32[]{:S(2)}) collective-permute-start(f32[2,4,32]{2,1,0:T(4,128)S(1)} %fusion.92), channel_id=1, source_target_pairs={{0,8},{4,12},{8,0},{12,4},{1,9},{5,13},{9,1},{13,5},{2,10},{6,14},... | collective-permute-start | bytes 3080 | tf_op jit(solution)/shard_map/ppermute | solution.py:36
  126.1 2.4 collective-permute-done.10
  128.6 2.8 %collective-permute-start.11 = (f32[2,4,32]{2,1,0:T(4,128)S(1)}, f32[2,4,32]{2,1,0:T(4,128)S(1)}, u32[]{:S(2)}, u32[]{:S(2)}) collective-permute-start(f32[2,4,32]{2,1,0:T(4,128)S(1)} %fusion.103), channel_id=1, source_target_pairs={{0,1},{1,0},{2,3},{3,2},{4,5},{5,4},{6,7},{7,6},{8,9},{9,8},{10,11... | collective-permute-start | bytes 3080 | tf_op jit(solution)/shard_map/ppermute | solution.py:36
  133.2 3.7 %collective-permute-start.12 = (f32[2,4,32]{2,1,0:T(4,128)S(1)}, f32[2,4,32]{2,1,0:T(4,128)S(1)}, u32[]{:S(2)}, u32[]{:S(2)}) collective-permute-start(f32[2,4,32]{2,1,0:T(4,128)S(1)} %add.132), channel_id=1, source_target_pairs={{0,2},{1,3},{2,0},{3,1},{4,6},{5,7},{6,4},{7,5},{8,10},{9,11},{10,... | collective-permute-start | bytes 3080 | tf_op jit(solution)/shard_map/ppermute | solution.py:36
  136.9 2.4 collective-permute-done.12
  139.4 33.6 %all-to-all-done = bf16[32,4,16,256]{3,2,1,0:T(8,128)(2,1)S(1)} async-done(((bf16[32,4,16,256]{3,2,1,0:T(8,128)(2,1)}), bf16[32,4,16,256]{3,2,1,0:T(8,128)(2,1)S(1)}, u32[]{:S(2)}, u32[]{:S(2)}) %all-to-all-start) | async-done | bytes 1048608 | tf_op jit(solution)/shard_map/all_to_all | solution.py:121
  174.1 4.8 %all-to-all-start.1 = ((f32[32,8,1024]{2,1,0:T(8,128)}), f32[32,8,1024]{2,1,0:T(8,128)}, u32[]{:S(2)}, u32[]{:S(2)}) async-start(f32[32,8,1024]{2,1,0:T(8,128)} %stack.20), calls=%async_computation.1 | async-start | bytes 2097152 | tf_op jit(solution)/shard_map/all_to_all | solution.py:127
  179.3 55.4 %all-to-all-done.1 = f32[32,8,1024]{2,1,0:T(8,128)} async-done(((f32[32,8,1024]{2,1,0:T(8,128)}), f32[32,8,1024]{2,1,0:T(8,128)}, u32[]{:S(2)}, u32[]{:S(2)}) %all-to-all-start.1) | async-done | bytes 1048608 | tf_op jit(solution)/shard_map/all_to_all | solution.py:127
  236.1 4.6 %convolution_convert_fusion = bf16[128,16,768]{2,0,1:T(8,128)(2,1)} fusion(f32[128,16,256]{2,1,0:T(8,128)S(1)} %bitcast_convert_fusion, f32[256]{0:T(256)S(1)} %bitcast.149, f32[128,256]{1,0:T(8,128)S(1)} %copy.54, f32[128,256]{1,0:T(8,128)S(1)} %copy.52, bf16[256,4096]{1,0:T(8,128)(2,1)} %all-gather.2.cloned.1.call-done), kind=kOutput, calls=%fused_computation.7 | convolution fusion | flops 808976384 | bytes 5899264 | tf_op jit(solution)/shard_map/fpc,cd->fpd/dot_general | solution.py:132
  240.8 2.1 fusion.97
  242.9 3.9 %fusion.31 = bf16[1,1,16,128,256]{4,3,2,1,0:T(8,128)(2,1)} fusion(f32[128,16,256]{2,1,0:T(8,128)S(1)} %bitcast_convert_fusion, bf16[128,16,768]{2,0,1:T(8,128)(2,1)} %convolution_convert_fusion, f32[16,128,128]{1,2,0:T(8,128)S(1)} %get-tuple-element.24, f32[16,128]{1,0:T(8,128)S(1)} %get-tuple-element.23, bf16[256,4096]{1,0:T(8,128)(2,1)} %all-gather.2.cloned.1.call-done), kind=kOutput, calls=%fused_computation.39 | convolution fusion | flops 404750336 | bytes 5382144 | tf_op jit(solution)/shard_map/axi,iy->axy/dot_general | solution.py:150
  (91 shorter events, 37.1 us)
Async XLA Ops:
  6.5 25.2 %copy-start.1 = (bf16[4,16,32,256]{3,2,1,0:T(8,128)(2,1)S(1)}, bf16[4,16,32,256]{3,2,1,0:T(8,128)(2,1)}, u32[]{:S(2)}) copy-start(bf16[4,16,32,256]{3,2,1,0:T(8,128)(2,1)} %param.7) | copy-start | bytes 3145732
  6.5 68.1 %all-gather.2.cloned.1.call-start = ((), (), s32[]{:S(2)}) async-start(), calls=%async_computation.2 | async-start | bytes 2228224 | tf_op jit(solution)/shard_map/all_gather | solution.py:76
  10.2 5.0 %collective-permute-start = (f32[2,4,32]{2,1,0:T(4,128)S(1)}, f32[2,4,32]{2,1,0:T(4,128)S(1)}, u32[]{:S(2)}, u32[]{:S(2)}) collective-permute-start(f32[2,4,32]{2,1,0:T(4,128)S(1)} %pad_maximum_fusion.6), channel_id=1, source_target_pairs={{0,4},{4,0},{8,12},{12,8},{1,5},{5,1},{9,13},{13,9},{2,6},{6,2},{1... | collective-permute-start | bytes 3080 | tf_op jit(solution)/shard_map/ppermute | solution.py:36
  15.2 6.0 %collective-permute-start.1 = (f32[2,4,32]{2,1,0:T(4,128)S(1)}, f32[2,4,32]{2,1,0:T(4,128)S(1)}, u32[]{:S(2)}, u32[]{:S(2)}) collective-permute-start(f32[2,4,32]{2,1,0:T(4,128)S(1)} %fusion.93), channel_id=1, source_target_pairs={{0,8},{4,12},{8,0},{12,4},{1,9},{5,13},{9,1},{13,5},{2,10},{6,14},... | collective-permute-start | bytes 3080 | tf_op jit(solution)/shard_map/ppermute | solution.py:36
  21.2 4.3 %collective-permute-start.2 = (f32[2,4,32]{2,1,0:T(4,128)S(1)}, f32[2,4,32]{2,1,0:T(4,128)S(1)}, u32[]{:S(2)}, u32[]{:S(2)}) collective-permute-start(f32[2,4,32]{2,1,0:T(4,128)S(1)} %fusion.104), channel_id=1, source_target_pairs={{0,1},{1,0},{2,3},{3,2},{4,5},{5,4},{6,7},{7,6},{8,9},{9,8},{10,11... | collective-permute-start | bytes 3080 | tf_op jit(solution)/shard_map/ppermute | solution.py:36
  25.5 5.8 %collective-permute-start.3 = (f32[2,4,32]{2,1,0:T(4,128)S(1)}, f32[2,4,32]{2,1,0:T(4,128)S(1)}, u32[]{:S(2)}, u32[]{:S(2)}) collective-permute-start(f32[2,4,32]{2,1,0:T(4,128)S(1)} %add.111), channel_id=1, source_target_pairs={{0,2},{1,3},{2,0},{3,1},{4,6},{5,7},{6,4},{7,5},{8,10},{9,11},{10,... | collective-permute-start | bytes 3080 | tf_op jit(solution)/shard_map/ppermute | solution.py:36
  32.4 4.6 %collective-permute-start.4 = (bf16[4,1,32,256]{3,2,1,0:T(8,128)(2,1)S(1)}, bf16[4,1,32,256]{3,2,1,0:T(8,128)(2,1)S(1)}, u32[]{:S(2)}, u32[]{:S(2)}) collective-permute-start(bf16[4,1,32,256]{3,2,1,0:T(8,128)(2,1)S(1)} %get-tuple-element.13), channel_id=1, source_target_pairs={{0,4},{4,8},{8,12},{1,5},{5,9},{9,13},{2,6},{6,10},{10,14},{3,7},{... | collective-permute-start | bytes 196616 | tf_op jit(solution)/shard_map/ppermute | solution.py:18
  35.7 5.4 %collective-permute-start.5 = (bf16[4,1,32,256]{3,2,1,0:T(8,128)(2,1)S(1)}, bf16[4,1,32,256]{3,2,1,0:T(8,128)(2,1)S(1)}, u32[]{:S(2)}, u32[]{:S(2)}) collective-permute-start(bf16[4,1,32,256]{3,2,1,0:T(8,128)(2,1)S(1)} %get-tuple-element.14), channel_id=1, source_target_pairs={{4,0},{8,4},{12,8},{5,1},{9,5},{13,9},{6,2},{10,6},{14,10},{7,3},{... | collective-permute-start | bytes 196616 | tf_op jit(solution)/shard_map/ppermute | solution.py:19
  41.3 4.6 %collective-permute-start.6 = (bf16[4,18,1,256]{3,2,1,0:T(2,128)(2,1)S(1)}, bf16[4,18,1,256]{3,2,1,0:T(2,128)(2,1)S(1)}, u32[]{:S(2)}, u32[]{:S(2)}) collective-permute-start(bf16[4,18,1,256]{3,2,1,0:T(2,128)(2,1)S(1)} %get-tuple-element.12), channel_id=1, source_target_pairs={{0,1},{1,2},{2,3},{4,5},{5,6},{6,7},{8,9},{9,10},{10,11},{12,13},{... | collective-permute-start | bytes 110600 | tf_op jit(solution)/shard_map/ppermute | solution.py:18
  44.5 5.1 %collective-permute-start.7 = (bf16[4,18,1,256]{3,2,1,0:T(2,128)(2,1)S(1)}, bf16[4,18,1,256]{3,2,1,0:T(2,128)(2,1)S(1)}, u32[]{:S(2)}, u32[]{:S(2)}) collective-permute-start(bf16[4,18,1,256]{3,2,1,0:T(2,128)(2,1)S(1)} %get-tuple-element.11), channel_id=1, source_target_pairs={{1,0},{2,1},{3,2},{5,4},{6,5},{7,6},{9,8},{10,9},{11,10},{13,12},{... | collective-permute-start | bytes 110600 | tf_op jit(solution)/shard_map/ppermute | solution.py:19
  74.6 1.7 copy-start.3
  76.3 1.4 copy-start
  80.4 6.4 %copy-start.4 = (s32[16]{0:T(128)S(1)}, s32[16]{0:T(128)}, u32[]{:S(2)}) copy-start(s32[16]{0:T(128)} %param.8) | copy-start | bytes 196
  81.5 11.4 %collective-permute-start.8 = (bf16[2,16,32,256]{3,2,1,0:T(8,128)(2,1)S(1)}, bf16[2,16,32,256]{3,2,1,0:T(8,128)(2,1)S(1)}, u32[]{:S(2)}, u32[]{:S(2)}) collective-permute-start(bf16[2,16,32,256]{3,2,1,0:T(8,128)(2,1)S(1)} %slice.197), channel_id=1, source_target_pairs={{0,16},{16,32},{32,48},{48,64},{64,80},{80,96},{96,112},{112,128},... | collective-permute-start | bytes 1572872 | tf_op jit(solution)/shard_map/ppermute | solution.py:27
  98.0 1.4 copy-start.2
  102.3 70.8 %all-to-all-start = ((bf16[32,4,16,256]{3,2,1,0:T(8,128)(2,1)}), bf16[32,4,16,256]{3,2,1,0:T(8,128)(2,1)S(1)}, u32[]{:S(2)}, u32[]{:S(2)}) async-start(bf16[32,4,16,256]{3,2,1,0:T(8,128)(2,1)} %bitcast.134), calls=%async_computation | async-start | bytes 2097152 | tf_op jit(solution)/shard_map/all_to_all | solution.py:121
  117.8 4.6 %collective-permute-start.9 = (f32[2,4,32]{2,1,0:T(4,128)S(1)}, f32[2,4,32]{2,1,0:T(4,128)S(1)}, u32[]{:S(2)}, u32[]{:S(2)}) collective-permute-start(f32[2,4,32]{2,1,0:T(4,128)S(1)} %pad_maximum_fusion.7), channel_id=1, source_target_pairs={{0,4},{4,0},{8,12},{12,8},{1,5},{5,1},{9,13},{13,9},{2,6},{6,2},{1... | collective-permute-start | bytes 3080 | tf_op jit(solution)/shard_map/ppermute | solution.py:36
  122.4 6.1 %collective-permute-start.10 = (f32[2,4,32]{2,1,0:T(4,128)S(1)}, f32[2,4,32]{2,1,0:T(4,128)S(1)}, u32[]{:S(2)}, u32[]{:S(2)}) collective-permute-start(f32[2,4,32]{2,1,0:T(4,128)S(1)} %fusion.92), channel_id=1, source_target_pairs={{0,8},{4,12},{8,0},{12,4},{1,9},{5,13},{9,1},{13,5},{2,10},{6,14},... | collective-permute-start | bytes 3080 | tf_op jit(solution)/shard_map/ppermute | solution.py:36
  128.6 4.6 %collective-permute-start.11 = (f32[2,4,32]{2,1,0:T(4,128)S(1)}, f32[2,4,32]{2,1,0:T(4,128)S(1)}, u32[]{:S(2)}, u32[]{:S(2)}) collective-permute-start(f32[2,4,32]{2,1,0:T(4,128)S(1)} %fusion.103), channel_id=1, source_target_pairs={{0,1},{1,0},{2,3},{3,2},{4,5},{5,4},{6,7},{7,6},{8,9},{9,8},{10,11... | collective-permute-start | bytes 3080 | tf_op jit(solution)/shard_map/ppermute | solution.py:36
  133.2 6.1 %collective-permute-start.12 = (f32[2,4,32]{2,1,0:T(4,128)S(1)}, f32[2,4,32]{2,1,0:T(4,128)S(1)}, u32[]{:S(2)}, u32[]{:S(2)}) collective-permute-start(f32[2,4,32]{2,1,0:T(4,128)S(1)} %add.132), channel_id=1, source_target_pairs={{0,2},{1,3},{2,0},{3,1},{4,6},{5,7},{6,4},{7,5},{8,10},{9,11},{10,... | collective-permute-start | bytes 3080 | tf_op jit(solution)/shard_map/ppermute | solution.py:36
  174.1 60.6 %all-to-all-start.1 = ((f32[32,8,1024]{2,1,0:T(8,128)}), f32[32,8,1024]{2,1,0:T(8,128)}, u32[]{:S(2)}, u32[]{:S(2)}) async-start(f32[32,8,1024]{2,1,0:T(8,128)} %stack.20), calls=%async_computation.1 | async-start | bytes 2097152 | tf_op jit(solution)/shard_map/all_to_all | solution.py:127
Sparse Core Ops, SparseCore 0:
  10.3 64.2 all-gather.1
